TPU v7x, 256 devices: a whole 4x4x8 slice. The times are simulated.
256 devices in a mesh: ctx: 32 (over y_hi, z, core), uly: 8 (over x, y_lo).
Axes of the slice: x: 4, y: 4 (y_hi: 2, y_lo: 2; y = y_hi * 2 + y_lo), z: 8, core: 2. Of those that a mesh axis runs over, the one named last changes fastest.
Arguments:
- queries: bfloat16 [32768, 4096], P(('ctx', 'uly')), may hold values from -200 to 200, as said below
- keys: bfloat16 [32768, 1024], P(('ctx', 'uly')), may hold values from -6 to 6, as said below
- values: bfloat16 [32768, 1024], P(('ctx', 'uly')), may hold values from -6 to 6
Outputs:
- attended: bfloat16 [32768, 4096], P(('ctx', 'uly'))
Inputs may be any that keep to these rules, and one draw needn't show every extreme that they name: `queries`: entries of order one, except that some query rows may be large. `keys`: entries of order one.
All inputs are finite; a program needn't handle non-finite values.
Results may differ from a plain program's by a relative error of at most 0.0055.
Values may be sent and summed in bfloat16 or wider, within the bound.
No kernel may reach another device: no remote copies, remote signals or barrier semaphores. Data moves between devices by JAX's collectives and lax.ppermute only.
A program may use at most 64 MiB of HBM per device.

v0:
```python
import functools

import jax
import jax.numpy as jnp
from jax import lax
from jax.experimental import pallas as pl
from jax.experimental.pallas import tpu as pltpu
from jax.sharding import PartitionSpec as P


HEAD_SIZE = 128
WINDOW_BLOCKS = 3
KEY_TILE = 1024
LOG2_E = 1.4426950408889634


def passed_along(block, axis, distance):
    devices = range(lax.axis_size(axis))
    route = [(i - distance, i) for i in devices if i - distance in devices]
    return lax.ppermute(block, axis, route)


def attend_kernel(pos_ref, q_ref, kv_ref, *refs, block_len, back, last):
    if last:
        parts = [refs[3 * i:3 * i + 3] for i in range(WINDOW_BLOCKS)]
        o_ref = refs[3 * WINDOW_BLOCKS]
        m_ref, l_ref, acc_ref = refs[3 * WINDOW_BLOCKS + 1:]
    else:
        m_ref, l_ref, acc_ref = refs
    cycle_pos = pos_ref[0]
    exp_scale = HEAD_SIZE ** (-0.5) * LOG2_E
    tile = min(KEY_TILE, block_len)

    def process(start, masked, fresh):
        q = q_ref[...]
        k = kv_ref[pl.ds(start, tile), pl.ds(0, HEAD_SIZE)]
        v = kv_ref[pl.ds(start, tile), pl.ds(HEAD_SIZE, HEAD_SIZE)]
        s = lax.dot_general(k, q, (((1,), (1,)), ((), ())), preferred_element_type=jnp.float32)
        if masked:
            keys = lax.broadcasted_iota(jnp.int32, s.shape, 0) + start
            rows = lax.broadcasted_iota(jnp.int32, s.shape, 1)
            s = jnp.where(keys <= rows, s, jnp.float32(-1e30))
        if fresh:
            m_new = jnp.max(s, axis=0, keepdims=True)
        else:
            m_old = m_ref[...]
            m_new = jnp.maximum(m_old, jnp.max(s, axis=0, keepdims=True))
        p = jnp.exp2((s - m_new) * exp_scale)
        pv = lax.dot_general(
            v, p.astype(jnp.bfloat16), (((0,), (0,)), ((), ())), preferred_element_type=jnp.float32
        )
        if fresh:
            l_ref[...] = jnp.sum(p, axis=0, keepdims=True)
            acc_ref[...] = pv
        else:
            factor = jnp.exp2((m_old - m_new) * exp_scale)
            l_ref[...] = l_ref[...] * factor + jnp.sum(p, axis=0, keepdims=True)
            acc_ref[...] = acc_ref[...] * factor + pv
        m_ref[...] = m_new

    starts = [t * tile for t in range(block_len // tile)]
    if back == 0:
        for j, start in enumerate(starts):
            process(start, True, j == 0)
    else:
        for j, start in enumerate(starts):
            process(start, False, j == 0)

    if last:
        states = [(r[0][...], r[1][...], r[2][...]) for r in parts] + [(m_ref[...], l_ref[...], acc_ref[...])]
        seen = [cycle_pos >= b for b in range(len(states))]
        m_all = states[0][0]
        for b in range(1, len(states)):
            m_all = jnp.maximum(m_all, jnp.where(seen[b], states[b][0], -jnp.inf))
        total = jnp.zeros_like(m_all)
        acc = jnp.zeros(acc_ref.shape, jnp.float32)
        for b, (m_b, l_b, acc_b) in enumerate(states):
            factor = jnp.exp2((m_b - m_all) * exp_scale)
            total = total + jnp.where(seen[b], l_b * factor, 0.0)
            acc = acc + jnp.where(seen[b], acc_b * factor, 0.0)
        o_ref[...] = (acc / total).T.astype(o_ref.dtype)


def attend(pos, q_src, kv, kv_col, q_heads, back, parts=None):
    block_len = q_src.shape[0]
    last = parts is not None
    kernel = functools.partial(attend_kernel, block_len=block_len, back=back, last=last)
    row_spec = pl.BlockSpec((None, 1, block_len), lambda h, pos: (h, 0, 0))
    acc_spec = pl.BlockSpec((None, HEAD_SIZE, block_len), lambda h, pos: (h, 0, 0))
    in_specs = [
        pl.BlockSpec((block_len, HEAD_SIZE), lambda h, pos: (0, h)),
        pl.BlockSpec((block_len, 2 * HEAD_SIZE), lambda h, pos: (0, kv_col)),
    ]
    operands = [pos, q_src, kv]
    state_shapes = [
        jax.ShapeDtypeStruct((q_heads, 1, block_len), jnp.float32),
        jax.ShapeDtypeStruct((q_heads, 1, block_len), jnp.float32),
        jax.ShapeDtypeStruct((q_heads, HEAD_SIZE, block_len), jnp.float32),
    ]
    if last:
        for part in parts:
            in_specs += [row_spec, row_spec, acc_spec]
            operands += list(part)
        out_specs = pl.BlockSpec((block_len, HEAD_SIZE), lambda h, pos: (0, h))
        out_shape = jax.ShapeDtypeStruct((block_len, q_heads * HEAD_SIZE), jnp.bfloat16)
        scratch = [
            pltpu.VMEM((1, block_len), jnp.float32),
            pltpu.VMEM((1, block_len), jnp.float32),
            pltpu.VMEM((HEAD_SIZE, block_len), jnp.float32),
        ]
    else:
        out_specs = [row_spec, row_spec, acc_spec]
        out_shape = state_shapes
        scratch = []
    grid_spec = pltpu.PrefetchScalarGridSpec(
        num_scalar_prefetch=1,
        grid=(q_heads,),
        in_specs=in_specs,
        out_specs=out_specs,
        scratch_shapes=scratch,
    )
    return pl.pallas_call(
        kernel,
        grid_spec=grid_spec,
        out_shape=out_shape,
        compiler_params=pltpu.CompilerParams(dimension_semantics=("arbitrary",)),
    )(*operands)


def on_device(queries, keys, values):
    n = lax.axis_size("uly")
    rows = queries.shape[0]
    cycle_pos = lax.axis_index("ctx")
    packed = jnp.concatenate(
        [queries.reshape(rows, n, -1), keys.reshape(rows, n, -1), values.reshape(rows, n, -1)], axis=2
    )
    qkv = lax.all_to_all(packed, "uly", split_axis=1, concat_axis=0, tiled=True)
    qkv = qkv.reshape(rows * n, -1)
    q_heads = (qkv.shape[1] - 2 * HEAD_SIZE) // HEAD_SIZE
    pos = jnp.reshape(cycle_pos, (1,)).astype(jnp.int32)
    kv_own = qkv[:, q_heads * HEAD_SIZE:]
    parts = [attend(pos, qkv, qkv, q_heads // 2, q_heads, 0)]
    for back in range(1, WINDOW_BLOCKS + 1):
        kv = passed_along(kv_own, "ctx", back)
        last = back == WINDOW_BLOCKS
        parts.append(attend(pos, qkv, kv, 0, q_heads, back, parts if last else None))
    return lax.all_to_all(parts[-1], "uly", split_axis=0, concat_axis=1, tiled=True)


def solution(mesh):
    placed = (P(("ctx", "uly"), None), P(("ctx", "uly"), None), P(("ctx", "uly"), None))
    return jax.shard_map(
        on_device, mesh=mesh, in_specs=placed, out_specs=P(("ctx", "uly"), None), check_vma=False
    )
```

profile of v0, /device:TPU:97, one launch (start us, length us, event | category | flops | bytes accessed | tf_op | source)
XLA Modules:
  0.0 99.0 jit_solution(14121287171161675146)
XLA Ops:
  0.0 0.0 copy-start
  0.0 0.0 copy-start.5
  0.0 1.4 %copy.15 = bf16[16,8,8,512]{3,2,0,1:T(8,128)(2,1)S(1)} copy(bf16[16,8,8,512]{3,2,1,0:T(8,128)(2,1)} %bitcast.33) | data formatting | bytes 2097152 | tf_op jit(solution)/shard_map/reshape | solution.py:135
  1.4 0.0 copy-done
  1.4 0.0 copy-done.5
  1.4 0.1 copy_bitcast_fusion.1
  1.5 0.1 pad_maximum_fusion
  1.7 24.9 %all_to_all.34 = bf16[128,8,768]{2,0,1:T(8,128)(2,1)S(1)} all-to-all(bf16[128,8,768]{2,0,1:T(8,128)(2,1)S(1)} %pad_maximum_fusion), channel_id=1, replica_groups=mesh['ctx'=32,'uly'=8] {'uly'}, dimensions={1} | all-to-all | bytes 3145728 | tf_op jit(solution)/shard_map/all_to_all | solution.py:137
  26.6 0.0 copy-start.1
  26.6 0.9 slice.4
  27.5 6.5 %collective-permute-start.1 = (bf16[1024,256]{1,0:T(8,128)(2,1)}, bf16[1024,256]{1,0:T(8,128)(2,1)S(1)}, u32[]{:S(2)}, u32[]{:S(2)}) collective-permute-start(bf16[1024,256]{1,0:T(8,128)(2,1)} %slice.4), channel_id=1, source_target_pairs={{0,8},{8,16},{16,24},{24,32},{32,40},{40,48},{48,56},{56,64},{64,7... | collective-permute-start | bytes 1572872 | tf_op jit(solution)/shard_map/ppermute | solution.py:20
  33.9 2.6 %collective-permute-start.2 = (bf16[1024,256]{1,0:T(8,128)(2,1)}, bf16[1024,256]{1,0:T(8,128)(2,1)S(1)}, u32[]{:S(2)}, u32[]{:S(2)}) collective-permute-start(bf16[1024,256]{1,0:T(8,128)(2,1)} %slice.4), channel_id=1, source_target_pairs={{0,16},{8,24},{16,32},{24,40},{32,48},{40,56},{48,64},{56,72},{64,... | collective-permute-start | bytes 1572872 | tf_op jit(solution)/shard_map/ppermute | solution.py:20
  36.6 2.7 %collective-permute-start = (bf16[1024,256]{1,0:T(8,128)(2,1)}, bf16[1024,256]{1,0:T(8,128)(2,1)S(1)}, u32[]{:S(2)}, u32[]{:S(2)}) collective-permute-start(bf16[1024,256]{1,0:T(8,128)(2,1)} %slice.4), channel_id=1, source_target_pairs={{0,24},{8,32},{16,40},{24,48},{32,56},{40,64},{48,72},{56,80},{64,... | collective-permute-start | bytes 1572872 | tf_op jit(solution)/shard_map/ppermute | solution.py:20
  39.3 0.0 copy-done.1
  39.3 7.0 %shard_map.37 = (f32[4,1,1024]{2,1,0:T(1,128)}, f32[4,1,1024]{2,1,0:T(1,128)}, f32[4,128,1024]{2,1,0:T(8,128)}) custom-call(s32[1]{0:T(128)} %bitcast.pos_ref, bf16[1024,768]{1,0:T(8,128)(2,1)} %bitcast.25, bf16[1024,768]{1,0:T(8,128)(2,1)} %bitcast.26), custom_call_target="tpu_custom_call" | custom-call | tf_op jit(solution)/shard_map/pallas_call | solution.py:122
  46.3 0.0 collective-permute-done.1.kv_ref
  46.3 0.0 copy-start.4
  46.3 0.8 copy-done.4
  47.1 8.8 %shard_map.38 = (f32[4,1,1024]{2,1,0:T(1,128)}, f32[4,1,1024]{2,1,0:T(1,128)}, f32[4,128,1024]{2,1,0:T(8,128)}) custom-call(s32[1]{0:T(128)} %bitcast.pos_ref, bf16[1024,768]{1,0:T(8,128)(2,1)} %bitcast.27, bf16[1024,256]{1,0:T(8,128)(2,1)} %copy-done.4), custom_call_target="tpu_custom_call" | custom-call | tf_op jit(solution)/shard_map/pallas_call | solution.py:122
  55.9 0.0 collective-permute-done.2.kv_ref
  55.9 0.0 copy-start.3
  55.9 0.8 copy-done.3
  56.8 8.8 %shard_map.39 = (f32[4,1,1024]{2,1,0:T(1,128)}, f32[4,1,1024]{2,1,0:T(1,128)}, f32[4,128,1024]{2,1,0:T(8,128)}) custom-call(s32[1]{0:T(128)} %bitcast.pos_ref, bf16[1024,768]{1,0:T(8,128)(2,1)} %bitcast.28, bf16[1024,256]{1,0:T(8,128)(2,1)} %copy-done.3), custom_call_target="tpu_custom_call" | custom-call | tf_op jit(solution)/shard_map/pallas_call | solution.py:122
  65.6 2.8 %collective-permute-done.kv_ref = bf16[1024,256]{1,0:T(8,128)(2,1)S(1)} collective-permute-done((bf16[1024,256]{1,0:T(8,128)(2,1)}, bf16[1024,256]{1,0:T(8,128)(2,1)S(1)}, u32[]{:S(2)}, u32[]{:S(2)}) %collective-permute-start) | collective-permute-done | bytes 524320 | tf_op jit(solution)/shard_map/ppermute | solution.py:20
  68.5 0.0 copy-start.2
  68.5 0.8 copy-done.2
  69.3 10.2 %shard_map.40 = bf16[1024,512]{1,0:T(8,128)(2,1)} custom-call(s32[1]{0:T(128)} %bitcast.pos_ref, bf16[1024,768]{1,0:T(8,128)(2,1)} %bitcast.29, bf16[1024,256]{1,0:T(8,128)(2,1)} %copy-done.2, f32[4,1,1024]{2,1,0:T(1,128)} %get-tuple-element.14.refs_0_, f32[4,1,1024]{2,1,0:T(1,128)} %get-tuple-element.15.refs_1_, f32[4,128,1024]{2,1,0:T(8,128)} %get-tuple-element.16.refs_2_, ...), custom_call_target="tpu_custom_call" | custom-call | tf_op jit(solution)/shard_map/pallas_call | solution.py:122
  79.5 18.5 %all_to_all.35 = bf16[8,128,512]{2,1,0:T(8,128)(2,1)S(1)} all-to-all(bf16[8,128,512]{2,1,0:T(8,128)(2,1)} %bitcast.30), channel_id=1, replica_groups=mesh['ctx'=32,'uly'=8] {'uly'}, dimensions={0} | all-to-all | bytes 2097152 | tf_op jit(solution)/shard_map/all_to_all | solution.py:147
  97.9 1.1 %copy.11 = bf16[8,16,8,512]{3,2,0,1:T(8,128)(2,1)} copy(bf16[8,16,8,512]{3,2,1,0:T(8,128)(2,1)S(1)} %bitcast.32) | data formatting | bytes 2097152 | tf_op jit(solution)/shard_map/all_to_all | solution.py:147
Async XLA Ops:
  0.0 1.4 %copy-start = (bf16[128,1024]{1,0:T(8,128)(2,1)S(1)}, bf16[128,1024]{1,0:T(8,128)(2,1)}, u32[]{:S(2)}) copy-start(bf16[128,1024]{1,0:T(8,128)(2,1)} %param.4) | copy-start | bytes 786436
  0.0 1.4 %copy-start.5 = (bf16[128,1024]{1,0:T(8,128)(2,1)S(1)}, bf16[128,1024]{1,0:T(8,128)(2,1)}, u32[]{:S(2)}) copy-start(bf16[128,1024]{1,0:T(8,128)(2,1)} %param.5) | copy-start | bytes 786436
  26.6 12.7 %copy-start.1 = (bf16[128,8,768]{2,0,1:T(8,128)(2,1)}, bf16[128,8,768]{2,0,1:T(8,128)(2,1)S(1)}, u32[]{:S(2)}) copy-start(bf16[128,8,768]{2,0,1:T(8,128)(2,1)S(1)} %all_to_all.34) | copy-start | bytes 4718596
  27.5 18.8 %collective-permute-start.1 = (bf16[1024,256]{1,0:T(8,128)(2,1)}, bf16[1024,256]{1,0:T(8,128)(2,1)S(1)}, u32[]{:S(2)}, u32[]{:S(2)}) collective-permute-start(bf16[1024,256]{1,0:T(8,128)(2,1)} %slice.4), channel_id=1, source_target_pairs={{0,8},{8,16},{16,24},{24,32},{32,40},{40,48},{48,56},{56,64},{64,7... | collective-permute-start | bytes 1572872 | tf_op jit(solution)/shard_map/ppermute | solution.py:20
  33.9 22.0 %collective-permute-start.2 = (bf16[1024,256]{1,0:T(8,128)(2,1)}, bf16[1024,256]{1,0:T(8,128)(2,1)S(1)}, u32[]{:S(2)}, u32[]{:S(2)}) collective-permute-start(bf16[1024,256]{1,0:T(8,128)(2,1)} %slice.4), channel_id=1, source_target_pairs={{0,16},{8,24},{16,32},{24,40},{32,48},{40,56},{48,64},{56,72},{64,... | collective-permute-start | bytes 1572872 | tf_op jit(solution)/shard_map/ppermute | solution.py:20
  36.6 31.9 %collective-permute-start = (bf16[1024,256]{1,0:T(8,128)(2,1)}, bf16[1024,256]{1,0:T(8,128)(2,1)S(1)}, u32[]{:S(2)}, u32[]{:S(2)}) collective-permute-start(bf16[1024,256]{1,0:T(8,128)(2,1)} %slice.4), channel_id=1, source_target_pairs={{0,24},{8,32},{16,40},{24,48},{32,56},{40,64},{48,72},{56,80},{64,... | collective-permute-start | bytes 1572872 | tf_op jit(solution)/shard_map/ppermute | solution.py:20
  46.3 0.8 copy-start.4
  55.9 0.8 copy-start.3
  68.5 0.8 copy-start.2
where the time goes:
time: 99.4 us; the launch traced here: 99 us
  blocking collectives  43.4 us (44%)
  Pallas kernels  34.9 us (35%)
  starting transfers between devices  11.8 us (12%)
  local copies, waits for them, and re-layouts  5.94 us (6%)
  waiting for transfers between devices  2.83 us (3%)
    pallas_call x4, Pallas kernels, attend(): pl.pallas_call(kernel, grid_spec=grid_spec, out_shape=out_shape, compiler...  34.9 us
    all_to_all x1, blocking collectives, on_device(): qkv = lax.all_to_all(packed, 'uly', split_axis=1, concat_axis=0, tiled=True)  24.9 us
    all_to_all x1, blocking collectives, on_device(): lax.all_to_all(parts[-1], 'uly', split_axis=0, concat_axis=1, tiled=True)  18.5 us
    ppermute x3, starting transfers between devices, passed_along(): return lax.ppermute(block, axis, route)  11.8 us
    ppermute x3, waiting for transfers between devices, passed_along(): return lax.ppermute(block, axis, route)  2.83 us
    unnamed x12, local copies, waits for them, and re-layouts  2.5 us
  transfers between devices with their start and end apart: 3, of which 1 were waited for; matrix products, arithmetic and copies ran while one was open for 0% of the time, Pallas kernels for 25%

commit v1 on v0

--- a/solution.py
+++ b/solution.py
@@ -45,7 +45,7 @@
         else:
             m_old = m_ref[...]
             m_new = jnp.maximum(m_old, jnp.max(s, axis=0, keepdims=True))
-        p = jnp.exp2((s - m_new) * exp_scale)
+        p = jnp.exp2(s * exp_scale - m_new * exp_scale)
         pv = lax.dot_general(
             v, p.astype(jnp.bfloat16), (((0,), (0,)), ((), ())), preferred_element_type=jnp.float32
         )
@@ -138,10 +138,10 @@
     qkv = qkv.reshape(rows * n, -1)
     q_heads = (qkv.shape[1] - 2 * HEAD_SIZE) // HEAD_SIZE
     pos = jnp.reshape(cycle_pos, (1,)).astype(jnp.int32)
-    kv_own = qkv[:, q_heads * HEAD_SIZE:]
+    kv = qkv[:, q_heads * HEAD_SIZE:]
     parts = [attend(pos, qkv, qkv, q_heads // 2, q_heads, 0)]
     for back in range(1, WINDOW_BLOCKS + 1):
-        kv = passed_along(kv_own, "ctx", back)
+        kv = passed_along(kv, "ctx", 1)
         last = back == WINDOW_BLOCKS
         parts.append(attend(pos, qkv, kv, 0, q_heads, back, parts if last else None))
     return lax.all_to_all(parts[-1], "uly", split_axis=0, concat_axis=1, tiled=True)

time: 99.4 us -> 113 us (1.14)
  waiting for transfers between devices: 2.83 us -> 12.2 us
  starting transfers between devices: 11.8 us -> 17.7 us
  Pallas kernels: 34.9 us -> 38 us
  local copies, waits for them, and re-layouts: 5.94 us -> 3.46 us
  blocking collectives: 43.4 us -> 41.3 us
    ppermute x3, waiting for transfers between devices: 2.83 us -> 12.2 us  [passed_along(): return lax.ppermute(block, axis, route)]
    ppermute x3, starting transfers between devices: 11.8 us -> 17.7 us  [passed_along(): return lax.ppermute(block, axis, route)]
    pallas_call x4, Pallas kernels: 34.9 us -> 38 us  [attend(): pl.pallas_call(kernel, grid_spec=grid_spec, out_shape=out_shape, compiler...]
    all_to_all x1, blocking collectives: 18.5 us -> 16.4 us  [on_device(): lax.all_to_all(parts[-1], 'uly', split_axis=0, concat_axis=1, tiled=True)]
    unnamed x12, local copies, waits for them, and re-layouts: 2.5 us -> 0.86 us
  transfers between devices with their start and end apart: 3 -> 3, of which waited for: 1 -> 2; matrix products, arithmetic and copies ran while one was open for 0% -> 0% of each run, Pallas kernels for 25% -> 24%
where the time goes in v1:
time: 113 us
  blocking collectives  41.3 us (37%)
  Pallas kernels  38 us (34%)
  starting transfers between devices  17.7 us (16%)
  waiting for transfers between devices  12.2 us (11%)
  local copies, waits for them, and re-layouts  3.46 us (3%)
    pallas_call x4, Pallas kernels, attend(): pl.pallas_call(kernel, grid_spec=grid_spec, out_shape=out_shape, compiler...  38 us
    all_to_all x1, blocking collectives, on_device(): qkv = lax.all_to_all(packed, 'uly', split_axis=1, concat_axis=0, tiled=True)  24.9 us
    ppermute x3, starting transfers between devices, passed_along(): return lax.ppermute(block, axis, route)  17.7 us
    all_to_all x1, blocking collectives, on_device(): lax.all_to_all(parts[-1], 'uly', split_axis=0, concat_axis=1, tiled=True)  16.4 us
    ppermute x3, waiting for transfers between devices, passed_along(): return lax.ppermute(block, axis, route)  12.2 us
  transfers between devices with their start and end apart: 3, of which 2 were waited for; matrix products, arithmetic and copies ran while one was open for 0% of the time, Pallas kernels for 24%

profile of v1, /device:TPU:97, one launch (start us, length us, event | category | flops | bytes accessed | tf_op | source)
XLA Modules:
  0.0 112.8 jit_solution(6607640288266284438)
XLA Ops:
  0.0 0.0 copy-start
  0.0 0.0 copy-start.5
  0.0 1.4 %copy.15 = bf16[16,8,8,512]{3,2,0,1:T(8,128)(2,1)S(1)} copy(bf16[16,8,8,512]{3,2,1,0:T(8,128)(2,1)} %bitcast.33) | data formatting | bytes 2097152 | tf_op jit(solution)/shard_map/reshape | solution.py:135
  1.4 0.0 copy-done
  1.4 0.0 copy-done.5
  1.4 0.1 copy_bitcast_fusion.1
  1.5 0.1 pad_maximum_fusion
  1.7 24.9 %all_to_all.34 = bf16[128,8,768]{2,0,1:T(8,128)(2,1)S(1)} all-to-all(bf16[128,8,768]{2,0,1:T(8,128)(2,1)S(1)} %pad_maximum_fusion), channel_id=1, replica_groups=mesh['ctx'=32,'uly'=8] {'uly'}, dimensions={1} | all-to-all | bytes 3145728 | tf_op jit(solution)/shard_map/all_to_all | solution.py:137
  26.6 0.0 copy-start.1
  26.6 6.5 %collective-permute-start = (bf16[1024,256]{1,0:T(8,128)(2,1)S(1)}, bf16[1024,256]{1,0:T(8,128)(2,1)S(1)}, u32[]{:S(2)}, u32[]{:S(2)}) collective-permute-start(bf16[1024,256]{1,0:T(8,128)(2,1)S(1)} %slice.4), channel_id=1, source_target_pairs={{0,8},{8,16},{16,24},{24,32},{32,40},{40,48},{48,56},{56,64},{64,7... | collective-permute-start | bytes 1572872 | tf_op jit(solution)/shard_map/ppermute | solution.py:20
  33.1 6.1 %collective-permute-done.kv_ref = bf16[1024,256]{1,0:T(8,128)(2,1)S(1)} collective-permute-done((bf16[1024,256]{1,0:T(8,128)(2,1)S(1)}, bf16[1024,256]{1,0:T(8,128)(2,1)S(1)}, u32[]{:S(2)}, u32[]{:S(2)}) %collective-permute-start) | collective-permute-done | bytes 524320 | tf_op jit(solution)/shard_map/ppermute | solution.py:20
  39.2 0.0 copy-start.2
  39.2 5.6 %collective-permute-start.1 = (bf16[1024,256]{1,0:T(8,128)(2,1)S(1)}, bf16[1024,256]{1,0:T(8,128)(2,1)S(1)}, u32[]{:S(2)}, u32[]{:S(2)}) collective-permute-start(bf16[1024,256]{1,0:T(8,128)(2,1)S(1)} %collective-permute-done.kv_ref), channel_id=1, source_target_pairs={{0,8},{8,16},{16,24},{24,32},{32,40},{40,48},{48,56},{56,64},{64,7... | collective-permute-start | bytes 1572872 | tf_op jit(solution)/shard_map/ppermute | solution.py:20
  44.8 6.1 %collective-permute-done.1.kv_ref = bf16[1024,256]{1,0:T(8,128)(2,1)S(1)} collective-permute-done((bf16[1024,256]{1,0:T(8,128)(2,1)S(1)}, bf16[1024,256]{1,0:T(8,128)(2,1)S(1)}, u32[]{:S(2)}, u32[]{:S(2)}) %collective-permute-start.1) | collective-permute-done | bytes 524320 | tf_op jit(solution)/shard_map/ppermute | solution.py:20
  50.9 0.0 copy-start.4
  50.9 5.6 %collective-permute-start.2 = (bf16[1024,256]{1,0:T(8,128)(2,1)S(1)}, bf16[1024,256]{1,0:T(8,128)(2,1)S(1)}, u32[]{:S(2)}, u32[]{:S(2)}) collective-permute-start(bf16[1024,256]{1,0:T(8,128)(2,1)S(1)} %collective-permute-done.1.kv_ref), channel_id=1, source_target_pairs={{0,8},{8,16},{16,24},{24,32},{32,40},{40,48},{48,56},{56,64},{64,7... | collective-permute-start | bytes 1572872 | tf_op jit(solution)/shard_map/ppermute | solution.py:20
  56.5 0.0 copy-done.1
  56.5 7.4 %shard_map.37 = (f32[4,1,1024]{2,1,0:T(1,128)}, f32[4,1,1024]{2,1,0:T(1,128)}, f32[4,128,1024]{2,1,0:T(8,128)}) custom-call(s32[1]{0:T(128)} %bitcast.pos_ref, bf16[1024,768]{1,0:T(8,128)(2,1)} %bitcast.25, bf16[1024,768]{1,0:T(8,128)(2,1)} %bitcast.26), custom_call_target="tpu_custom_call" | custom-call | tf_op jit(solution)/shard_map/pallas_call | solution.py:122
  63.9 0.0 copy-done.2
  63.9 9.7 %shard_map.38 = (f32[4,1,1024]{2,1,0:T(1,128)}, f32[4,1,1024]{2,1,0:T(1,128)}, f32[4,128,1024]{2,1,0:T(8,128)}) custom-call(s32[1]{0:T(128)} %bitcast.pos_ref, bf16[1024,768]{1,0:T(8,128)(2,1)} %bitcast.27, bf16[1024,256]{1,0:T(8,128)(2,1)} %copy-done.2), custom_call_target="tpu_custom_call" | custom-call | tf_op jit(solution)/shard_map/pallas_call | solution.py:122
  73.7 0.0 copy-done.4
  73.7 9.7 %shard_map.39 = (f32[4,1,1024]{2,1,0:T(1,128)}, f32[4,1,1024]{2,1,0:T(1,128)}, f32[4,128,1024]{2,1,0:T(8,128)}) custom-call(s32[1]{0:T(128)} %bitcast.pos_ref, bf16[1024,768]{1,0:T(8,128)(2,1)} %bitcast.28, bf16[1024,256]{1,0:T(8,128)(2,1)} %copy-done.4), custom_call_target="tpu_custom_call" | custom-call | tf_op jit(solution)/shard_map/pallas_call | solution.py:122
  83.4 0.0 collective-permute-done.2.kv_ref
  83.4 0.0 copy-start.3
  83.4 0.8 copy-done.3
  84.3 11.1 %shard_map.40 = bf16[1024,512]{1,0:T(8,128)(2,1)} custom-call(s32[1]{0:T(128)} %bitcast.pos_ref, bf16[1024,768]{1,0:T(8,128)(2,1)} %bitcast.29, bf16[1024,256]{1,0:T(8,128)(2,1)} %copy-done.3, f32[4,1,1024]{2,1,0:T(1,128)} %get-tuple-element.14.refs_0_, f32[4,1,1024]{2,1,0:T(1,128)} %get-tuple-element.15.refs_1_, f32[4,128,1024]{2,1,0:T(8,128)} %get-tuple-element.16.refs_2_, ...), custom_call_target="tpu_custom_call" | custom-call | tf_op jit(solution)/shard_map/pallas_call | solution.py:122
  95.4 16.4 %all_to_all.35 = bf16[8,128,512]{2,1,0:T(8,128)(2,1)S(1)} all-to-all(bf16[8,128,512]{2,1,0:T(8,128)(2,1)} %bitcast.30), channel_id=1, replica_groups=mesh['ctx'=32,'uly'=8] {'uly'}, dimensions={0} | all-to-all | bytes 2097152 | tf_op jit(solution)/shard_map/all_to_all | solution.py:147
  111.7 1.1 copy.11
  (1 shorter events, 0.0 us)
Async XLA Ops:
  0.0 1.4 %copy-start = (bf16[128,1024]{1,0:T(8,128)(2,1)S(1)}, bf16[128,1024]{1,0:T(8,128)(2,1)}, u32[]{:S(2)}) copy-start(bf16[128,1024]{1,0:T(8,128)(2,1)} %param.4) | copy-start | bytes 786436
  0.0 1.4 %copy-start.5 = (bf16[128,1024]{1,0:T(8,128)(2,1)S(1)}, bf16[128,1024]{1,0:T(8,128)(2,1)}, u32[]{:S(2)}) copy-start(bf16[128,1024]{1,0:T(8,128)(2,1)} %param.5) | copy-start | bytes 786436
  26.6 29.9 %copy-start.1 = (bf16[128,8,768]{2,0,1:T(8,128)(2,1)}, bf16[128,8,768]{2,0,1:T(8,128)(2,1)S(1)}, u32[]{:S(2)}) copy-start(bf16[128,8,768]{2,0,1:T(8,128)(2,1)S(1)} %all_to_all.34) | copy-start | bytes 4718596
  26.6 12.6 %collective-permute-start = (bf16[1024,256]{1,0:T(8,128)(2,1)S(1)}, bf16[1024,256]{1,0:T(8,128)(2,1)S(1)}, u32[]{:S(2)}, u32[]{:S(2)}) collective-permute-start(bf16[1024,256]{1,0:T(8,128)(2,1)S(1)} %slice.4), channel_id=1, source_target_pairs={{0,8},{8,16},{16,24},{24,32},{32,40},{40,48},{48,56},{56,64},{64,7... | collective-permute-start | bytes 1572872 | tf_op jit(solution)/shard_map/ppermute | solution.py:20
  39.2 24.7 %copy-start.2 = (bf16[1024,256]{1,0:T(8,128)(2,1)}, bf16[1024,256]{1,0:T(8,128)(2,1)S(1)}, u32[]{:S(2)}) copy-start(bf16[1024,256]{1,0:T(8,128)(2,1)S(1)} %collective-permute-done.kv_ref) | copy-start | bytes 1572868
  39.2 11.7 %collective-permute-start.1 = (bf16[1024,256]{1,0:T(8,128)(2,1)S(1)}, bf16[1024,256]{1,0:T(8,128)(2,1)S(1)}, u32[]{:S(2)}, u32[]{:S(2)}) collective-permute-start(bf16[1024,256]{1,0:T(8,128)(2,1)S(1)} %collective-permute-done.kv_ref), channel_id=1, source_target_pairs={{0,8},{8,16},{16,24},{24,32},{32,40},{40,48},{48,56},{56,64},{64,7... | collective-permute-start | bytes 1572872 | tf_op jit(solution)/shard_map/ppermute | solution.py:20
  50.9 22.7 %copy-start.4 = (bf16[1024,256]{1,0:T(8,128)(2,1)}, bf16[1024,256]{1,0:T(8,128)(2,1)S(1)}, u32[]{:S(2)}) copy-start(bf16[1024,256]{1,0:T(8,128)(2,1)S(1)} %collective-permute-done.1.kv_ref) | copy-start | bytes 1572868
  50.9 32.5 %collective-permute-start.2 = (bf16[1024,256]{1,0:T(8,128)(2,1)S(1)}, bf16[1024,256]{1,0:T(8,128)(2,1)S(1)}, u32[]{:S(2)}, u32[]{:S(2)}) collective-permute-start(bf16[1024,256]{1,0:T(8,128)(2,1)S(1)} %collective-permute-done.1.kv_ref), channel_id=1, source_target_pairs={{0,8},{8,16},{16,24},{24,32},{32,40},{40,48},{48,56},{56,64},{64,7... | collective-permute-start | bytes 1572872 | tf_op jit(solution)/shard_map/ppermute | solution.py:20
  83.4 0.8 copy-start.3

commit v2 on v1

--- a/solution.py
+++ b/solution.py
@@ -45,7 +45,7 @@
         else:
             m_old = m_ref[...]
             m_new = jnp.maximum(m_old, jnp.max(s, axis=0, keepdims=True))
-        p = jnp.exp2(s * exp_scale - m_new * exp_scale)
+        p = jnp.exp2((s - m_new) * exp_scale)
         pv = lax.dot_general(
             v, p.astype(jnp.bfloat16), (((0,), (0,)), ((), ())), preferred_element_type=jnp.float32
         )
@@ -58,10 +58,38 @@
             acc_ref[...] = acc_ref[...] * factor + pv
         m_ref[...] = m_new
 
+    def process_diag(start, width, q_lo, fresh):
+        q = q_ref[pl.ds(q_lo, block_len - q_lo), :]
+        k = kv_ref[pl.ds(start, width), pl.ds(0, HEAD_SIZE)]
+        v = kv_ref[pl.ds(start, width), pl.ds(HEAD_SIZE, HEAD_SIZE)]
+        s = lax.dot_general(k, q, (((1,), (1,)), ((), ())), preferred_element_type=jnp.float32)
+        keys = lax.broadcasted_iota(jnp.int32, s.shape, 0) + start
+        rows = lax.broadcasted_iota(jnp.int32, s.shape, 1) + q_lo
+        s = jnp.where(keys <= rows, s, jnp.float32(-1e30))
+        cols = pl.ds(q_lo, block_len - q_lo)
+        if fresh:
+            m_new = jnp.max(s, axis=0, keepdims=True)
+        else:
+            m_old = m_ref[:, cols]
+            m_new = jnp.maximum(m_old, jnp.max(s, axis=0, keepdims=True))
+        p = jnp.exp2((s - m_new) * exp_scale)
+        pv = lax.dot_general(
+            v, p.astype(jnp.bfloat16), (((0,), (0,)), ((), ())), preferred_element_type=jnp.float32
+        )
+        if fresh:
+            l_ref[...] = jnp.sum(p, axis=0, keepdims=True)
+            acc_ref[...] = pv
+        else:
+            factor = jnp.exp2((m_old - m_new) * exp_scale)
+            l_ref[:, cols] = l_ref[:, cols] * factor + jnp.sum(p, axis=0, keepdims=True)
+            acc_ref[:, cols] = acc_ref[:, cols] * factor + pv
+        m_ref[:, cols] = m_new
+
     starts = [t * tile for t in range(block_len // tile)]
     if back == 0:
-        for j, start in enumerate(starts):
-            process(start, True, j == 0)
+        half = block_len // 2
+        process_diag(0, half, 0, True)
+        process_diag(half, half, half, False)
     else:
         for j, start in enumerate(starts):
             process(start, False, j == 0)

time: 113 us -> 110 us (0.973)
  Pallas kernels: 38 us -> 35.1 us
    pallas_call x4, Pallas kernels: 38 us -> 35.1 us  [attend(): pl.pallas_call(kernel, grid_spec=grid_spec, out_shape=out_shape, compiler...]
  transfers between devices with their start and end apart: 3 -> 3, of which waited for: 2 -> 2; matrix products, arithmetic and copies ran while one was open for 0% -> 0% of each run, Pallas kernels for 24% -> 23%
where the time goes in v2:
time: 110 us
  blocking collectives  41.3 us (38%)
  Pallas kernels  35.1 us (32%)
  starting transfers between devices  17.7 us (16%)
  waiting for transfers between devices  12.2 us (11%)
  local copies, waits for them, and re-layouts  3.46 us (3%)
    pallas_call x4, Pallas kernels, attend(): pl.pallas_call(kernel, grid_spec=grid_spec, out_shape=out_shape, compiler...  35.1 us
    all_to_all x1, blocking collectives, on_device(): qkv = lax.all_to_all(packed, 'uly', split_axis=1, concat_axis=0, tiled=True)  24.9 us
    ppermute x3, starting transfers between devices, passed_along(): return lax.ppermute(block, axis, route)  17.7 us
    all_to_all x1, blocking collectives, on_device(): lax.all_to_all(parts[-1], 'uly', split_axis=0, concat_axis=1, tiled=True)  16.4 us
    ppermute x3, waiting for transfers between devices, passed_along(): return lax.ppermute(block, axis, route)  12.2 us
  transfers between devices with their start and end apart: 3, of which 2 were waited for; matrix products, arithmetic and copies ran while one was open for 0% of the time, Pallas kernels for 23%

profile of v2, /device:TPU:97, one launch (start us, length us, event | category | flops | bytes accessed | tf_op | source)
XLA Modules:
  0.0 109.9 jit_solution(1956258627406240790)
XLA Ops:
  0.0 0.0 copy-start
  0.0 0.0 copy-start.5
  0.0 1.4 %copy.15 = bf16[16,8,8,512]{3,2,0,1:T(8,128)(2,1)S(1)} copy(bf16[16,8,8,512]{3,2,1,0:T(8,128)(2,1)} %bitcast.33) | data formatting | bytes 2097152 | tf_op jit(solution)/shard_map/reshape | solution.py:163
  1.4 0.0 copy-done
  1.4 0.0 copy-done.5
  1.4 0.1 copy_bitcast_fusion.1
  1.5 0.1 pad_maximum_fusion
  1.7 24.9 %all_to_all.34 = bf16[128,8,768]{2,0,1:T(8,128)(2,1)S(1)} all-to-all(bf16[128,8,768]{2,0,1:T(8,128)(2,1)S(1)} %pad_maximum_fusion), channel_id=1, replica_groups=mesh['ctx'=32,'uly'=8] {'uly'}, dimensions={1} | all-to-all | bytes 3145728 | tf_op jit(solution)/shard_map/all_to_all | solution.py:165
  26.6 0.0 copy-start.1
  26.6 6.5 %collective-permute-start = (bf16[1024,256]{1,0:T(8,128)(2,1)S(1)}, bf16[1024,256]{1,0:T(8,128)(2,1)S(1)}, u32[]{:S(2)}, u32[]{:S(2)}) collective-permute-start(bf16[1024,256]{1,0:T(8,128)(2,1)S(1)} %slice.4), channel_id=1, source_target_pairs={{0,8},{8,16},{16,24},{24,32},{32,40},{40,48},{48,56},{56,64},{64,7... | collective-permute-start | bytes 1572872 | tf_op jit(solution)/shard_map/ppermute | solution.py:20
  33.1 6.1 %collective-permute-done.kv_ref = bf16[1024,256]{1,0:T(8,128)(2,1)S(1)} collective-permute-done((bf16[1024,256]{1,0:T(8,128)(2,1)S(1)}, bf16[1024,256]{1,0:T(8,128)(2,1)S(1)}, u32[]{:S(2)}, u32[]{:S(2)}) %collective-permute-start) | collective-permute-done | bytes 524320 | tf_op jit(solution)/shard_map/ppermute | solution.py:20
  39.2 0.0 copy-start.2
  39.2 5.6 %collective-permute-start.1 = (bf16[1024,256]{1,0:T(8,128)(2,1)S(1)}, bf16[1024,256]{1,0:T(8,128)(2,1)S(1)}, u32[]{:S(2)}, u32[]{:S(2)}) collective-permute-start(bf16[1024,256]{1,0:T(8,128)(2,1)S(1)} %collective-permute-done.kv_ref), channel_id=1, source_target_pairs={{0,8},{8,16},{16,24},{24,32},{32,40},{40,48},{48,56},{56,64},{64,7... | collective-permute-start | bytes 1572872 | tf_op jit(solution)/shard_map/ppermute | solution.py:20
  44.8 6.1 %collective-permute-done.1.kv_ref = bf16[1024,256]{1,0:T(8,128)(2,1)S(1)} collective-permute-done((bf16[1024,256]{1,0:T(8,128)(2,1)S(1)}, bf16[1024,256]{1,0:T(8,128)(2,1)S(1)}, u32[]{:S(2)}, u32[]{:S(2)}) %collective-permute-start.1) | collective-permute-done | bytes 524320 | tf_op jit(solution)/shard_map/ppermute | solution.py:20
  50.9 0.0 copy-start.4
  50.9 5.6 %collective-permute-start.2 = (bf16[1024,256]{1,0:T(8,128)(2,1)S(1)}, bf16[1024,256]{1,0:T(8,128)(2,1)S(1)}, u32[]{:S(2)}, u32[]{:S(2)}) collective-permute-start(bf16[1024,256]{1,0:T(8,128)(2,1)S(1)} %collective-permute-done.1.kv_ref), channel_id=1, source_target_pairs={{0,8},{8,16},{16,24},{24,32},{32,40},{40,48},{48,56},{56,64},{64,7... | collective-permute-start | bytes 1572872 | tf_op jit(solution)/shard_map/ppermute | solution.py:20
  56.5 0.0 copy-done.1
  56.5 7.2 %shard_map.37 = (f32[4,1,1024]{2,1,0:T(1,128)}, f32[4,1,1024]{2,1,0:T(1,128)}, f32[4,128,1024]{2,1,0:T(8,128)}) custom-call(s32[1]{0:T(128)} %bitcast.pos_ref, bf16[1024,768]{1,0:T(8,128)(2,1)} %bitcast.25, bf16[1024,768]{1,0:T(8,128)(2,1)} %bitcast.26), custom_call_target="tpu_custom_call" | custom-call | tf_op jit(solution)/shard_map/pallas_call | solution.py:150
  63.7 0.0 copy-done.2
  63.7 8.9 %shard_map.38 = (f32[4,1,1024]{2,1,0:T(1,128)}, f32[4,1,1024]{2,1,0:T(1,128)}, f32[4,128,1024]{2,1,0:T(8,128)}) custom-call(s32[1]{0:T(128)} %bitcast.pos_ref, bf16[1024,768]{1,0:T(8,128)(2,1)} %bitcast.27, bf16[1024,256]{1,0:T(8,128)(2,1)} %copy-done.2), custom_call_target="tpu_custom_call" | custom-call | tf_op jit(solution)/shard_map/pallas_call | solution.py:150
  72.5 0.0 copy-done.4
  72.5 8.9 %shard_map.39 = (f32[4,1,1024]{2,1,0:T(1,128)}, f32[4,1,1024]{2,1,0:T(1,128)}, f32[4,128,1024]{2,1,0:T(8,128)}) custom-call(s32[1]{0:T(128)} %bitcast.pos_ref, bf16[1024,768]{1,0:T(8,128)(2,1)} %bitcast.28, bf16[1024,256]{1,0:T(8,128)(2,1)} %copy-done.4), custom_call_target="tpu_custom_call" | custom-call | tf_op jit(solution)/shard_map/pallas_call | solution.py:150
  81.4 0.0 collective-permute-done.2.kv_ref
  81.4 0.0 copy-start.3
  81.4 0.8 copy-done.3
  82.3 10.2 %shard_map.40 = bf16[1024,512]{1,0:T(8,128)(2,1)} custom-call(s32[1]{0:T(128)} %bitcast.pos_ref, bf16[1024,768]{1,0:T(8,128)(2,1)} %bitcast.29, bf16[1024,256]{1,0:T(8,128)(2,1)} %copy-done.3, f32[4,1,1024]{2,1,0:T(1,128)} %get-tuple-element.14.refs_0_, f32[4,1,1024]{2,1,0:T(1,128)} %get-tuple-element.15.refs_1_, f32[4,128,1024]{2,1,0:T(8,128)} %get-tuple-element.16.refs_2_, ...), custom_call_target="tpu_custom_call" | custom-call | tf_op jit(solution)/shard_map/pallas_call | solution.py:150
  92.4 16.4 %all_to_all.35 = bf16[8,128,512]{2,1,0:T(8,128)(2,1)S(1)} all-to-all(bf16[8,128,512]{2,1,0:T(8,128)(2,1)} %bitcast.30), channel_id=1, replica_groups=mesh['ctx'=32,'uly'=8] {'uly'}, dimensions={0} | all-to-all | bytes 2097152 | tf_op jit(solution)/shard_map/all_to_all | solution.py:175
  108.8 1.1 copy.11
  (1 shorter events, 0.0 us)
Async XLA Ops:
  0.0 1.4 %copy-start = (bf16[128,1024]{1,0:T(8,128)(2,1)S(1)}, bf16[128,1024]{1,0:T(8,128)(2,1)}, u32[]{:S(2)}) copy-start(bf16[128,1024]{1,0:T(8,128)(2,1)} %param.4) | copy-start | bytes 786436
  0.0 1.4 %copy-start.5 = (bf16[128,1024]{1,0:T(8,128)(2,1)S(1)}, bf16[128,1024]{1,0:T(8,128)(2,1)}, u32[]{:S(2)}) copy-start(bf16[128,1024]{1,0:T(8,128)(2,1)} %param.5) | copy-start | bytes 786436
  26.6 29.9 %copy-start.1 = (bf16[128,8,768]{2,0,1:T(8,128)(2,1)}, bf16[128,8,768]{2,0,1:T(8,128)(2,1)S(1)}, u32[]{:S(2)}) copy-start(bf16[128,8,768]{2,0,1:T(8,128)(2,1)S(1)} %all_to_all.34) | copy-start | bytes 4718596
  26.6 12.6 %collective-permute-start = (bf16[1024,256]{1,0:T(8,128)(2,1)S(1)}, bf16[1024,256]{1,0:T(8,128)(2,1)S(1)}, u32[]{:S(2)}, u32[]{:S(2)}) collective-permute-start(bf16[1024,256]{1,0:T(8,128)(2,1)S(1)} %slice.4), channel_id=1, source_target_pairs={{0,8},{8,16},{16,24},{24,32},{32,40},{40,48},{48,56},{56,64},{64,7... | collective-permute-start | bytes 1572872 | tf_op jit(solution)/shard_map/ppermute | solution.py:20
  39.2 24.5 %copy-start.2 = (bf16[1024,256]{1,0:T(8,128)(2,1)}, bf16[1024,256]{1,0:T(8,128)(2,1)S(1)}, u32[]{:S(2)}) copy-start(bf16[1024,256]{1,0:T(8,128)(2,1)S(1)} %collective-permute-done.kv_ref) | copy-start | bytes 1572868
  39.2 11.7 %collective-permute-start.1 = (bf16[1024,256]{1,0:T(8,128)(2,1)S(1)}, bf16[1024,256]{1,0:T(8,128)(2,1)S(1)}, u32[]{:S(2)}, u32[]{:S(2)}) collective-permute-start(bf16[1024,256]{1,0:T(8,128)(2,1)S(1)} %collective-permute-done.kv_ref), channel_id=1, source_target_pairs={{0,8},{8,16},{16,24},{24,32},{32,40},{40,48},{48,56},{56,64},{64,7... | collective-permute-start | bytes 1572872 | tf_op jit(solution)/shard_map/ppermute | solution.py:20
  50.9 21.6 %copy-start.4 = (bf16[1024,256]{1,0:T(8,128)(2,1)}, bf16[1024,256]{1,0:T(8,128)(2,1)S(1)}, u32[]{:S(2)}) copy-start(bf16[1024,256]{1,0:T(8,128)(2,1)S(1)} %collective-permute-done.1.kv_ref) | copy-start | bytes 1572868
  50.9 30.5 %collective-permute-start.2 = (bf16[1024,256]{1,0:T(8,128)(2,1)S(1)}, bf16[1024,256]{1,0:T(8,128)(2,1)S(1)}, u32[]{:S(2)}, u32[]{:S(2)}) collective-permute-start(bf16[1024,256]{1,0:T(8,128)(2,1)S(1)} %collective-permute-done.1.kv_ref), channel_id=1, source_target_pairs={{0,8},{8,16},{16,24},{24,32},{32,40},{40,48},{48,56},{56,64},{64,7... | collective-permute-start | bytes 1572872 | tf_op jit(solution)/shard_map/ppermute | solution.py:20
  81.4 0.8 copy-start.3
